TPU v7x, 512 devices: a whole 4x8x8 slice. The times are simulated.
512 devices in a mesh: depth: 32 (over y, x), lat: 16 (over z, core).
Axes of the slice: x: 4, y: 8, z: 8, core: 2. Of those that a mesh axis runs over, the one named last changes fastest.
Arguments:
- thermal_state: float32 [1024, 8, 2048], P('depth', None, 'lat'), may hold values from -5 to 5
- sideways_face_flux_factor: float32 [1024, 8, 2048], P('depth', None, 'lat'), may hold values from 1 to 10
- downward_face_flux_factor: float32 [1024, 8, 2048], P('depth', None, 'lat'), may hold values from 1 to 10
Outputs:
- final_temperature: float32 [1024, 8, 2048], P('depth', None, 'lat')
All inputs are finite; a program needn't handle non-finite values.
Results may differ from a plain program's by a relative error of at most 0.0013.
Values sent between devices are 32-bit elements; how exact they have to be, the bound alone decides.
No kernel may reach another device: no remote copies, remote signals or barrier semaphores. Data moves between devices by JAX's collectives and lax.ppermute only.
A program may use at most 64 MiB of HBM per device.

v0:
```python
import jax
import jax.numpy as jnp
from jax import lax
from jax.sharding import PartitionSpec as P

sideways_coupling_quotient = 20.0
ratio_z = 2000.0


def extended(x, sides, width):
    for axis, dim in sides:
        count, length = (lax.axis_size(axis), x.shape[dim])
        up = [(i, (i + 1) % count) for i in range(count - 1)]
        down = [(j, i) for i, j in up]
        last = lax.slice_in_dim(x, length - width, length, axis=dim)
        first = lax.slice_in_dim(x, 0, width, axis=dim)
        before = lax.ppermute(last, axis, up)
        after = lax.ppermute(first, axis, down)
        x = jnp.concatenate([before, x, after], axis=dim)
    return x


def from_behind(x, axis, by):
    count = lax.axis_size(axis)
    pairs = [(i, i + by) for i in range(count) if 0 <= i + by < count]
    return lax.ppermute(x, axis, pairs)


def take_rows(values, start, stop, axis_index):
    return lax.slice_in_dim(values, start, stop, axis=axis_index)


def moved(values, stride, axis_index, filler, forward):
    count = values.shape[axis_index]
    pad_shape = list(values.shape)
    pad_shape[axis_index] = stride
    padding = jnp.full(pad_shape, filler, values.dtype)
    if forward:
        return jnp.concatenate(
            [take_rows(values, stride, count, axis_index), padding], axis=axis_index
        )
    return jnp.concatenate(
        [padding, take_rows(values, 0, count - stride, axis_index)], axis=axis_index
    )


def level_update(lower_band, diagonal, upper_band, rights, below, above):
    alpha_term = -lower_band / below[1]
    gamma_term = -upper_band / above[1]
    new_diagonal = diagonal + alpha_term * below[2] + gamma_term * above[0]
    new_rights = tuple(
        (
            column + alpha_term * low_col + gamma_term * high_col
            for column, low_col, high_col in zip(rights, below[3], above[3])
        )
    )
    return (alpha_term * below[0], new_diagonal, gamma_term * above[2], new_rights)


def cyclic(lower_band, diagonal, upper_band, rights, axis_index):
    count = lower_band.shape[axis_index]
    stride = 1
    while stride < count:
        below = (
            moved(lower_band, stride, axis_index, 0.0, False),
            moved(diagonal, stride, axis_index, 1.0, False),
            moved(upper_band, stride, axis_index, 0.0, False),
            tuple((moved(column, stride, axis_index, 0.0, False) for column in rights)),
        )
        above = (
            moved(lower_band, stride, axis_index, 0.0, True),
            moved(diagonal, stride, axis_index, 1.0, True),
            moved(upper_band, stride, axis_index, 0.0, True),
            tuple((moved(column, stride, axis_index, 0.0, True) for column in rights)),
        )
        lower_band, diagonal, upper_band, rights = level_update(
            lower_band, diagonal, upper_band, rights, below, above
        )
        stride = stride * 2
    return tuple((column / diagonal for column in rights))


def partition_solve(lower_band, upper_inner, rights, axis_index, fetch_next, reduced, fetch_prev):
    count = lower_band.shape[axis_index]
    inner_lower = take_rows(lower_band, 0, count - 1, axis_index)
    diagonal = 1.0 - inner_lower - upper_inner
    positions = lax.broadcasted_iota(jnp.int32, inner_lower.shape, axis_index)
    first_lower = take_rows(inner_lower, 0, 1, axis_index)
    last_upper = take_rows(upper_inner, count - 2, count - 1, axis_index)
    solve_lower = jnp.where(positions == 0, 0.0, inner_lower)
    solve_upper = jnp.where(positions == count - 2, 0.0, upper_inner)
    from_prev = jnp.where(positions == 0, -first_lower, 0.0)
    from_next = jnp.where(positions == count - 2, -last_upper, 0.0)
    inner_rights = take_rows(rights, 0, count - 1, axis_index)
    local_part, prev_part, next_part = cyclic(
        solve_lower, diagonal, solve_upper, (inner_rights, from_prev, from_next), axis_index
    )
    heads = (
        take_rows(local_part, 0, 1, axis_index),
        take_rows(prev_part, 0, 1, axis_index),
        take_rows(next_part, 0, 1, axis_index),
    )
    head_local, head_prev, head_next, last_coupling = fetch_next(heads)
    tail_local = take_rows(local_part, count - 2, count - 1, axis_index)
    tail_prev = take_rows(prev_part, count - 2, count - 1, axis_index)
    tail_next = take_rows(next_part, count - 2, count - 1, axis_index)
    lower_last = take_rows(lower_band, count - 1, count, axis_index)
    right_last = take_rows(rights, count - 1, count, axis_index)
    coeff_lower = lower_last * tail_prev
    coeff_diag = (
        1.0 - lower_last - last_coupling + lower_last * tail_next + last_coupling * head_prev
    )
    coeff_upper = last_coupling * head_next
    coeff_right = right_last - lower_last * tail_local - last_coupling * head_local
    interface_value = reduced(coeff_lower, coeff_diag, coeff_upper, coeff_right)
    previous = fetch_prev(interface_value)
    inner_values = local_part + prev_part * previous + next_part * interface_value
    return jnp.concatenate([inner_values, interface_value], axis=axis_index)


def on_device(thermal_state, sideways_face_flux_factor, downward_face_flux_factor):
    sideways_node_count = thermal_state.shape[2]
    grouped_sweep_rows = jnp.stack([thermal_state, sideways_face_flux_factor])
    padded = extended(grouped_sweep_rows, (("lat", 3),), 1)
    initial_operand_swapped = padded[0, :, :, :sideways_node_count]
    source_vector_swapped = padded[0, :, :, 2:]
    source_vector_downward = padded[1, :, :, 2:]
    known_operator_term = thermal_state + sideways_coupling_quotient * (
        source_vector_downward * (source_vector_swapped - thermal_state)
        - sideways_face_flux_factor * (thermal_state - initial_operand_swapped)
    )

    def depth_next(heads):
        arrived = from_behind(
            (heads[0], heads[1], heads[2], downward_face_flux_factor[0:1]), "depth", -1
        )
        return (arrived[0], arrived[1], arrived[2], -ratio_z * arrived[3])

    def depth_reduced(coeff_lower, coeff_diag, coeff_upper, coeff_right):
        gathered = (
            lax.all_gather(coeff_lower, "depth", axis=0, tiled=True),
            lax.all_gather(coeff_diag, "depth", axis=0, tiled=True),
            lax.all_gather(coeff_upper, "depth", axis=0, tiled=True),
            lax.all_gather(coeff_right, "depth", axis=0, tiled=True),
        )
        solved = cyclic(gathered[0], gathered[1], gathered[2], (gathered[3],), 0)[0]
        return lax.dynamic_slice_in_dim(solved, lax.axis_index("depth"), 1, 0)

    def depth_prev(interface_value):
        return from_behind(interface_value, "depth", 1)

    half_step = partition_solve(
        -ratio_z * downward_face_flux_factor,
        -ratio_z * downward_face_flux_factor[1:],
        known_operator_term,
        0,
        depth_next,
        depth_reduced,
        depth_prev,
    )
    reflected = 2.0 * half_step - known_operator_term
    lines = lax.all_to_all(reflected, "lat", split_axis=0, concat_axis=2, tiled=True)
    conduct_lines = lax.all_to_all(
        sideways_face_flux_factor, "lat", split_axis=0, concat_axis=2, tiled=True
    )
    lower_band = -sideways_coupling_quotient * conduct_lines
    upper_band = -sideways_coupling_quotient * jnp.concatenate(
        [conduct_lines[:, :, 1:], jnp.zeros_like(conduct_lines[:, :, :1])], axis=2
    )
    diagonal = 1.0 - lower_band - upper_band
    solve_lower = jnp.concatenate(
        [jnp.zeros_like(lower_band[:, :, :1]), lower_band[:, :, 1:]], axis=2
    )
    solved = cyclic(solve_lower, diagonal, upper_band, (lines,), 2)[0]
    return lax.all_to_all(solved, "lat", split_axis=2, concat_axis=0, tiled=True)


def solution(mesh):
    in_specs = (P("depth", None, "lat"), P("depth", None, "lat"), P("depth", None, "lat"))
    out_specs = P("depth", None, "lat")
    return jax.shard_map(
        on_device, mesh=mesh, in_specs=in_specs, out_specs=out_specs, check_vma=False
    )
```

profile of v0, /device:TPU:1, one launch (start us, length us, event | category | flops | bytes accessed | tf_op | source)
XLA Modules:
  0.0 245.1 jit_solution(14447107847641421287)
XLA Ops:
  0.0 1.3 slice_maximum_fusion
  1.3 8.8 %collective-permute-start = (f32[2,32,8,1]{3,2,1,0:T(8,128)S(1)}, f32[2,32,8,1]{3,2,1,0:T(8,128)S(1)}, u32[]{:S(2)}, u32[]{:S(2)}) collective-permute-start(f32[2,32,8,1]{3,2,1,0:T(8,128)S(1)} %get-tuple-element.67), channel_id=1, source_target_pairs={{1,0},{2,1},{3,2},{4,3},{5,4},{6,5},{7,6},{8,7},{9,8},{10,9},{11,1... | collective-permute-start | bytes 6152 | tf_op jit(solution)/shard_map/ppermute | solution.py:18
  10.1 1.9 collective-permute-start.1
  12.0 0.7 slice.672
  12.7 1.3 collective-permute-start.2
  14.0 0.9 broadcast_multiply_fusion.1
  14.9 0.9 slice_multiply_fusion
  15.9 1.2 fusion.5
  18.8 1.3 collective-permute-start.3
  20.3 1.3 collective-permute-start.4
  21.6 2.2 collective-permute-done.3
  23.8 2.1 collective-permute-done.4
  25.9 1.3 collective-permute-start.5
  27.2 34.0 %all_gather.13 = f32[32,8,128]{2,1,0:T(8,128)S(1)} all-gather(f32[1,8,128]{2,1,0:T(8,128)S(1)} %get-tuple-element.205), channel_id=1, replica_groups=mesh['depth'=32,'lat'=16] {'depth'}, dimensions={0}, use_global_device_ids=true | all-gather | bytes 135168 | tf_op jit(solution)/shard_map/all_gather | solution.py:141
  61.2 28.5 %all_gather.14 = f32[32,8,128]{2,1,0:T(8,128)S(1)} all-gather(f32[1,8,128]{2,1,0:T(8,128)S(1)} %get-tuple-element.84), channel_id=1, replica_groups=mesh['depth'=32,'lat'=16] {'depth'}, dimensions={0}, use_global_device_ids=true | all-gather | bytes 135168 | tf_op jit(solution)/shard_map/all_gather | solution.py:142
  89.7 28.7 %all_gather.12 = f32[32,8,128]{2,1,0:T(8,128)S(1)} all-gather(f32[1,8,128]{2,1,0:T(8,128)S(1)} %get-tuple-element.85), channel_id=1, replica_groups=mesh['depth'=32,'lat'=16] {'depth'}, dimensions={0}, use_global_device_ids=true | all-gather | bytes 135168 | tf_op jit(solution)/shard_map/all_gather | solution.py:144
  118.4 29.4 %all_gather.15 = f32[32,8,128]{2,1,0:T(8,128)S(1)} all-gather(f32[1,8,128]{2,1,0:T(8,128)S(1)} %multiply_multiply_fusion), channel_id=1, replica_groups=mesh['depth'=32,'lat'=16] {'depth'}, dimensions={0}, use_global_device_ids=true | all-gather | bytes 135168 | tf_op jit(solution)/shard_map/all_gather | solution.py:143
  148.9 1.7 collective-permute-start.6
  150.6 44.6 %all-to-all-start.1 = ((f32[32,8,128]{2,1,0:T(8,128)}), f32[32,8,128]{2,1,0:T(8,128)S(1)}, u32[]{:S(2)}, u32[]{:S(2)}) async-start(f32[32,8,128]{2,1,0:T(8,128)} %param.4), calls=%async_computation.1 | async-start | bytes 262144 | tf_op jit(solution)/shard_map/all_to_all | solution.py:163
  195.3 0.7 fusion.9
  195.9 8.5 %all-to-all-done.1 = f32[32,8,128]{2,1,0:T(8,128)S(1)} async-done(((f32[32,8,128]{2,1,0:T(8,128)}), f32[32,8,128]{2,1,0:T(8,128)S(1)}, u32[]{:S(2)}, u32[]{:S(2)}) %all-to-all-start.1) | async-done | bytes 131104 | tf_op jit(solution)/shard_map/all_to_all | solution.py:163
  204.4 3.6 %all-to-all-start = ((f32[32,8,128]{2,1,0:T(8,128)}), f32[32,8,128]{2,1,0:T(8,128)S(1)}, u32[]{:S(2)}, u32[]{:S(2)}) async-start(f32[32,8,128]{2,1,0:T(8,128)} %fusion.9), calls=%async_computation | async-start | bytes 262144 | tf_op jit(solution)/shard_map/all_to_all | solution.py:162
  208.6 7.8 %all-to-all-done = f32[32,8,128]{2,1,0:T(8,128)S(1)} async-done(((f32[32,8,128]{2,1,0:T(8,128)}), f32[32,8,128]{2,1,0:T(8,128)S(1)}, u32[]{:S(2)}, u32[]{:S(2)}) %all-to-all-start) | async-done | bytes 131104 | tf_op jit(solution)/shard_map/all_to_all | solution.py:162
  217.0 0.2 multiply_add_fusion.17
  217.8 0.2 multiply_add_fusion.15
  222.4 1.0 copy.11
  223.4 3.3 %reshape = f32[16,1,2048]{2,1,0:T(1,128)S(1)} reshape(f32[2048,2,8]{2,1,0:T(2,128)S(1)} %bitcast.51) | data formatting | bytes 262144
  226.8 11.8 %all_to_all.54 = f32[16,1,2048]{2,1,0:T(1,128)S(1)} all-to-all(f32[16,1,2048]{2,1,0:T(1,128)S(1)} %reshape), channel_id=1, replica_groups=mesh['depth'=32,'lat'=16] {'lat'}, dimensions={0} | all-to-all | bytes 262144 | tf_op jit(solution)/shard_map/all_to_all | solution.py:175
  238.6 0.5 broadcast.435
  239.1 0.9 reduce
  240.1 3.2 %reshape.1 = f32[2048,2,8]{2,1,0:T(2,128)S(1)} reshape(f32[16,2048]{1,0:T(8,128)S(1)} %reduce) | data formatting | bytes 262144
  243.2 1.9 copy.15
  (152 shorter events, 8.2 us)
Async XLA Ops:
  0.0 15.9 %copy-start = (f32[32,8,128]{2,1,0:T(8,128)S(1)}, f32[32,8,128]{2,1,0:T(8,128)}, u32[]{:S(2)}) copy-start(f32[32,8,128]{2,1,0:T(8,128)} %param.3) | copy-start | bytes 393220
  0.0 17.2 %copy-start.1 = (f32[32,8,128]{2,1,0:T(8,128)S(1)}, f32[32,8,128]{2,1,0:T(8,128)}, u32[]{:S(2)}) copy-start(f32[32,8,128]{2,1,0:T(8,128)} %param.5) | copy-start | bytes 393220
  1.3 14.6 %collective-permute-start = (f32[2,32,8,1]{3,2,1,0:T(8,128)S(1)}, f32[2,32,8,1]{3,2,1,0:T(8,128)S(1)}, u32[]{:S(2)}, u32[]{:S(2)}) collective-permute-start(f32[2,32,8,1]{3,2,1,0:T(8,128)S(1)} %get-tuple-element.67), channel_id=1, source_target_pairs={{1,0},{2,1},{3,2},{4,3},{5,4},{6,5},{7,6},{8,7},{9,8},{10,9},{11,1... | collective-permute-start | bytes 6152 | tf_op jit(solution)/shard_map/ppermute | solution.py:18
  10.1 5.8 %collective-permute-start.1 = (f32[2,32,8,1]{3,2,1,0:T(8,128)S(1)}, f32[2,32,8,1]{3,2,1,0:T(8,128)S(1)}, u32[]{:S(2)}, u32[]{:S(2)}) collective-permute-start(f32[2,32,8,1]{3,2,1,0:T(8,128)S(1)} %get-tuple-element.68), channel_id=1, source_target_pairs={{0,1},{1,2},{2,3},{3,4},{4,5},{5,6},{6,7},{7,8},{8,9},{9,10},{10,1... | collective-permute-start | bytes 6152 | tf_op jit(solution)/shard_map/ppermute | solution.py:17
  12.7 8.9 %collective-permute-start.2 = (f32[1,8,128]{2,1,0:T(8,128)S(1)}, f32[1,8,128]{2,1,0:T(8,128)S(1)}, u32[]{:S(2)}, u32[]{:S(2)}) collective-permute-start(f32[1,8,128]{2,1,0:T(8,128)S(1)} %slice.672), channel_id=1, source_target_pairs={{16,0},{32,16},{48,32},{64,48},{80,64},{96,80},{112,96},{128,112},... | collective-permute-start | bytes 12296 | tf_op jit(solution)/shard_map/ppermute | solution.py:26
  18.8 5.0 %collective-permute-start.3 = (f32[1,8,128]{2,1,0:T(8,128)S(1)}, f32[1,8,128]{2,1,0:T(8,128)S(1)}, u32[]{:S(2)}, u32[]{:S(2)}) collective-permute-start(f32[1,8,128]{2,1,0:T(8,128)S(1)} %slice.870), channel_id=1, source_target_pairs={{16,0},{32,16},{48,32},{64,48},{80,64},{96,80},{112,96},{128,112},... | collective-permute-start | bytes 12296 | tf_op jit(solution)/shard_map/ppermute | solution.py:26
  20.3 5.6 %collective-permute-start.4 = (f32[1,8,128]{2,1,0:T(8,128)S(1)}, f32[1,8,128]{2,1,0:T(8,128)S(1)}, u32[]{:S(2)}, u32[]{:S(2)}) collective-permute-start(f32[1,8,128]{2,1,0:T(8,128)S(1)} %slice.884), channel_id=1, source_target_pairs={{16,0},{32,16},{48,32},{64,48},{80,64},{96,80},{112,96},{128,112},... | collective-permute-start | bytes 12296 | tf_op jit(solution)/shard_map/ppermute | solution.py:26
  25.9 92.6 %collective-permute-start.5 = (f32[1,8,128]{2,1,0:T(8,128)S(1)}, f32[1,8,128]{2,1,0:T(8,128)S(1)}, u32[]{:S(2)}, u32[]{:S(2)}) collective-permute-start(f32[1,8,128]{2,1,0:T(8,128)S(1)} %get-tuple-element.212), channel_id=1, source_target_pairs={{16,0},{32,16},{48,32},{64,48},{80,64},{96,80},{112,96},{128,112},... | collective-permute-start | bytes 12296 | tf_op jit(solution)/shard_map/ppermute | solution.py:26
  148.9 46.3 %collective-permute-start.6 = (f32[1,8,128]{2,1,0:T(8,128)S(1)}, f32[1,8,128]{2,1,0:T(8,128)S(1)}, u32[]{:S(2)}, u32[]{:S(2)}) collective-permute-start(f32[1,8,128]{2,1,0:T(8,128)S(1)} %fusion.18), channel_id=1, source_target_pairs={{0,16},{16,32},{32,48},{48,64},{64,80},{80,96},{96,112},{112,128},... | collective-permute-start | bytes 12296 | tf_op jit(solution)/shard_map/ppermute | solution.py:26
  150.6 53.8 %all-to-all-start.1 = ((f32[32,8,128]{2,1,0:T(8,128)}), f32[32,8,128]{2,1,0:T(8,128)S(1)}, u32[]{:S(2)}, u32[]{:S(2)}) async-start(f32[32,8,128]{2,1,0:T(8,128)} %param.4), calls=%async_computation.1 | async-start | bytes 262144 | tf_op jit(solution)/shard_map/all_to_all | solution.py:163
  204.4 12.0 %all-to-all-start = ((f32[32,8,128]{2,1,0:T(8,128)}), f32[32,8,128]{2,1,0:T(8,128)S(1)}, u32[]{:S(2)}, u32[]{:S(2)}) async-start(f32[32,8,128]{2,1,0:T(8,128)} %fusion.9), calls=%async_computation | async-start | bytes 262144 | tf_op jit(solution)/shard_map/all_to_all | solution.py:162
where the time goes:
time: 246 us; the launch traced here: 245 us
  blocking collectives  132 us (54%)
  starting transfers between devices  65.8 us (27%)
  waiting for transfers between devices  20.6 us (8%)
  local copies, waits for them, and re-layouts  14.5 us (6%)
  other arithmetic  10.7 us (4%)
    all_to_all x1, starting transfers between devices, on_device(): lax.all_to_all(sideways_face_flux_factor, 'lat', split_axis=0, concat_axi...  44.6 us
    all_gather x1, blocking collectives, depth_reduced(): lax.all_gather(coeff_lower, 'depth', axis=0, tiled=True)  34 us
    all_gather x1, blocking collectives, depth_reduced(): lax.all_gather(coeff_upper, 'depth', axis=0, tiled=True)  29.4 us
    all_gather x1, blocking collectives, depth_reduced(): lax.all_gather(coeff_right, 'depth', axis=0, tiled=True)  28.7 us
    all_gather x1, blocking collectives, depth_reduced(): lax.all_gather(coeff_diag, 'depth', axis=0, tiled=True)  28.5 us
    all_to_all x1, blocking collectives, on_device(): lax.all_to_all(solved, 'lat', split_axis=2, concat_axis=0, tiled=True)  11.8 us
    ppermute x1, starting transfers between devices, extended(): after = lax.ppermute(first, axis, down)  8.79 us
    all_to_all x1, waiting for transfers between devices, on_device(): lax.all_to_all(sideways_face_flux_factor, 'lat', split_axis=0, concat_axi...  8.46 us
  transfers between devices with their start and end apart: 9, of which 4 were waited for; matrix products, arithmetic and copies ran while one was open for 3% of the time, Pallas kernels for 0%

commit v1 on v0

--- a/solution.py
+++ b/solution.py
@@ -172,7 +172,10 @@
         [jnp.zeros_like(lower_band[:, :, :1]), lower_band[:, :, 1:]], axis=2
     )
     solved = cyclic(solve_lower, diagonal, upper_band, (lines,), 2)[0]
-    return lax.all_to_all(solved, "lat", split_axis=2, concat_axis=0, tiled=True)
+    return jnp.concatenate(
+        lax.all_to_all(jnp.stack(jnp.split(solved, lax.axis_size("lat"), axis=2)), "lat", 0, 0),
+        axis=0,
+    )
 
 
 def solution(mesh):

time: 246 us -> 236 us (0.959)
  local copies, waits for them, and re-layouts: 14.5 us -> 4.56 us
  other arithmetic: 10.7 us -> 7.98 us
    unnamed x6 -> x20, local copies, waits for them, and re-layouts: 6.5 us -> 0.72 us
  transfers between devices with their start and end apart: 9 -> 9, of which waited for: 4 -> 5; matrix products, arithmetic and copies ran while one was open for 3% -> 2% of each run, Pallas kernels for 0% -> 0%
where the time goes in v1:
time: 236 us; the launch traced here: 235 us
  blocking collectives  132 us (56%)
  starting transfers between devices  67.2 us (28%)
  waiting for transfers between devices  21.9 us (9%)
  other arithmetic  7.98 us (3%)
  local copies, waits for them, and re-layouts  4.56 us (2%)
    all_to_all x1, starting transfers between devices, on_device(): lax.all_to_all(sideways_face_flux_factor, 'lat', split_axis=0, concat_axi...  46.2 us
    all_gather x1, blocking collectives, depth_reduced(): lax.all_gather(coeff_lower, 'depth', axis=0, tiled=True)  33.7 us
    all_gather x1, blocking collectives, depth_reduced(): lax.all_gather(coeff_upper, 'depth', axis=0, tiled=True)  29.3 us
    all_gather x1, blocking collectives, depth_reduced(): lax.all_gather(coeff_right, 'depth', axis=0, tiled=True)  28.8 us
    all_gather x1, blocking collectives, depth_reduced(): lax.all_gather(coeff_diag, 'depth', axis=0, tiled=True)  28.4 us
    all_to_all x1, blocking collectives, on_device(): lax.all_to_all(jnp.stack(jnp.split(solved, lax.axis_size('lat'), axis=2))...  11.9 us
    ppermute x1, starting transfers between devices, extended(): after = lax.ppermute(first, axis, down)  8.79 us
    all_to_all x1, waiting for transfers between devices, on_device(): lax.all_to_all(sideways_face_flux_factor, 'lat', split_axis=0, concat_axi...  8.46 us
  transfers between devices with their start and end apart: 9, of which 5 were waited for; matrix products, arithmetic and copies ran while one was open for 2% of the time, Pallas kernels for 0%

profile of v1, /device:TPU:1, one launch (start us, length us, event | category | flops | bytes accessed | tf_op | source)
XLA Modules:
  0.0 235.0 jit_solution(7500737944736265945)
XLA Ops:
  0.0 1.3 slice_maximum_fusion
  1.3 8.8 %collective-permute-start = (f32[2,32,8,1]{3,2,1,0:T(8,128)S(1)}, f32[2,32,8,1]{3,2,1,0:T(8,128)S(1)}, u32[]{:S(2)}, u32[]{:S(2)}) collective-permute-start(f32[2,32,8,1]{3,2,1,0:T(8,128)S(1)} %get-tuple-element.67), channel_id=1, source_target_pairs={{1,0},{2,1},{3,2},{4,3},{5,4},{6,5},{7,6},{8,7},{9,8},{10,9},{11,1... | collective-permute-start | bytes 6152 | tf_op jit(solution)/shard_map/ppermute | solution.py:18
  10.1 1.9 collective-permute-start.1
  12.0 1.3 collective-permute-start.2
  13.5 1.8 collective-permute-done.1
  15.3 1.2 fusion.5
  16.9 0.2 multiply_add_fusion.43
  17.3 0.2 multiply_add_fusion.41
  18.1 1.3 collective-permute-start.3
  19.6 1.3 collective-permute-start.4
  20.9 1.6 collective-permute-done.3
  22.5 2.1 collective-permute-done.4
  24.6 1.3 collective-permute-start.5
  25.9 33.7 %all_gather.13 = f32[32,8,128]{2,1,0:T(8,128)S(1)} all-gather(f32[1,8,128]{2,1,0:T(8,128)S(1)} %get-tuple-element.205), channel_id=1, replica_groups=mesh['depth'=32,'lat'=16] {'depth'}, dimensions={0}, use_global_device_ids=true | all-gather | bytes 135168 | tf_op jit(solution)/shard_map/all_gather | solution.py:141
  59.6 28.4 %all_gather.14 = f32[32,8,128]{2,1,0:T(8,128)S(1)} all-gather(f32[1,8,128]{2,1,0:T(8,128)S(1)} %get-tuple-element.84), channel_id=1, replica_groups=mesh['depth'=32,'lat'=16] {'depth'}, dimensions={0}, use_global_device_ids=true | all-gather | bytes 135168 | tf_op jit(solution)/shard_map/all_gather | solution.py:142
  88.1 28.8 %all_gather.12 = f32[32,8,128]{2,1,0:T(8,128)S(1)} all-gather(f32[1,8,128]{2,1,0:T(8,128)S(1)} %get-tuple-element.85), channel_id=1, replica_groups=mesh['depth'=32,'lat'=16] {'depth'}, dimensions={0}, use_global_device_ids=true | all-gather | bytes 135168 | tf_op jit(solution)/shard_map/all_gather | solution.py:144
  116.9 29.3 %all_gather.15 = f32[32,8,128]{2,1,0:T(8,128)S(1)} all-gather(f32[1,8,128]{2,1,0:T(8,128)S(1)} %multiply_multiply_fusion), channel_id=1, replica_groups=mesh['depth'=32,'lat'=16] {'depth'}, dimensions={0}, use_global_device_ids=true | all-gather | bytes 135168 | tf_op jit(solution)/shard_map/all_gather | solution.py:143
  147.3 1.7 collective-permute-start.6
  149.0 46.2 %all-to-all-start.1 = ((f32[32,8,128]{2,1,0:T(8,128)}), f32[32,8,128]{2,1,0:T(8,128)S(1)}, u32[]{:S(2)}, u32[]{:S(2)}) async-start(f32[32,8,128]{2,1,0:T(8,128)} %param.4), calls=%async_computation.1 | async-start | bytes 262144 | tf_op jit(solution)/shard_map/all_to_all | solution.py:163
  195.2 0.7 fusion.9
  195.9 8.5 %all-to-all-done.1 = f32[32,8,128]{2,1,0:T(8,128)S(1)} async-done(((f32[32,8,128]{2,1,0:T(8,128)}), f32[32,8,128]{2,1,0:T(8,128)S(1)}, u32[]{:S(2)}, u32[]{:S(2)}) %all-to-all-start.1) | async-done | bytes 131104 | tf_op jit(solution)/shard_map/all_to_all | solution.py:163
  204.4 3.4 %all-to-all-start = ((f32[32,8,128]{2,1,0:T(8,128)}), f32[32,8,128]{2,1,0:T(8,128)S(1)}, u32[]{:S(2)}, u32[]{:S(2)}) async-start(f32[32,8,128]{2,1,0:T(8,128)} %fusion.9), calls=%async_computation | async-start | bytes 262144 | tf_op jit(solution)/shard_map/all_to_all | solution.py:162
  208.3 8.0 %all-to-all-done = f32[32,8,128]{2,1,0:T(8,128)S(1)} async-done(((f32[32,8,128]{2,1,0:T(8,128)}), f32[32,8,128]{2,1,0:T(8,128)S(1)}, u32[]{:S(2)}, u32[]{:S(2)}) %all-to-all-start) | async-done | bytes 131104 | tf_op jit(solution)/shard_map/all_to_all | solution.py:162
  216.4 0.2 multiply_add_fusion.18
  216.9 0.2 multiply_add_fusion.17
  217.7 0.2 multiply_add_fusion.15
  218.4 0.2 multiply_add_fusion.13
  219.2 0.2 multiply_add_fusion.11
  220.0 0.2 multiply_add_fusion.9
  220.8 0.2 multiply_add_fusion.7
  222.5 11.9 %all_to_all.41 = f32[16,2,8,128]{3,2,1,0:T(8,128)S(1)} all-to-all(f32[16,2,8,128]{3,2,1,0:T(8,128)S(1)} %constant_dynamic-update-slice_fusion), channel_id=1, replica_groups=mesh['depth'=32,'lat'=16] {'lat'}, dimensions={0} | all-to-all | bytes 262144 | tf_op jit(solution)/shard_map/all_to_all | solution.py:176
  234.4 0.7 copy.33
  (162 shorter events, 6.9 us)
Async XLA Ops:
  0.0 12.0 %copy-start.1 = (f32[32,8,128]{2,1,0:T(8,128)S(1)}, f32[32,8,128]{2,1,0:T(8,128)}, u32[]{:S(2)}) copy-start(f32[32,8,128]{2,1,0:T(8,128)} %param.5) | copy-start | bytes 393220
  1.3 12.2 %collective-permute-start = (f32[2,32,8,1]{3,2,1,0:T(8,128)S(1)}, f32[2,32,8,1]{3,2,1,0:T(8,128)S(1)}, u32[]{:S(2)}, u32[]{:S(2)}) collective-permute-start(f32[2,32,8,1]{3,2,1,0:T(8,128)S(1)} %get-tuple-element.67), channel_id=1, source_target_pairs={{1,0},{2,1},{3,2},{4,3},{5,4},{6,5},{7,6},{8,7},{9,8},{10,9},{11,1... | collective-permute-start | bytes 6152 | tf_op jit(solution)/shard_map/ppermute | solution.py:18
  10.1 5.2 %collective-permute-start.1 = (f32[2,32,8,1]{3,2,1,0:T(8,128)S(1)}, f32[2,32,8,1]{3,2,1,0:T(8,128)S(1)}, u32[]{:S(2)}, u32[]{:S(2)}) collective-permute-start(f32[2,32,8,1]{3,2,1,0:T(8,128)S(1)} %get-tuple-element.68), channel_id=1, source_target_pairs={{0,1},{1,2},{2,3},{3,4},{4,5},{5,6},{6,7},{7,8},{8,9},{9,10},{10,1... | collective-permute-start | bytes 6152 | tf_op jit(solution)/shard_map/ppermute | solution.py:17
  12.0 8.9 %collective-permute-start.2 = (f32[1,8,128]{2,1,0:T(8,128)S(1)}, f32[1,8,128]{2,1,0:T(8,128)S(1)}, u32[]{:S(2)}, u32[]{:S(2)}) collective-permute-start(f32[1,8,128]{2,1,0:T(8,128)S(1)} %slice.672), channel_id=1, source_target_pairs={{16,0},{32,16},{48,32},{64,48},{80,64},{96,80},{112,96},{128,112},... | collective-permute-start | bytes 12296 | tf_op jit(solution)/shard_map/ppermute | solution.py:26
  13.4 1.9 copy-start
  18.1 4.4 %collective-permute-start.3 = (f32[1,8,128]{2,1,0:T(8,128)S(1)}, f32[1,8,128]{2,1,0:T(8,128)S(1)}, u32[]{:S(2)}, u32[]{:S(2)}) collective-permute-start(f32[1,8,128]{2,1,0:T(8,128)S(1)} %slice.870), channel_id=1, source_target_pairs={{16,0},{32,16},{48,32},{64,48},{80,64},{96,80},{112,96},{128,112},... | collective-permute-start | bytes 12296 | tf_op jit(solution)/shard_map/ppermute | solution.py:26
  19.6 5.0 %collective-permute-start.4 = (f32[1,8,128]{2,1,0:T(8,128)S(1)}, f32[1,8,128]{2,1,0:T(8,128)S(1)}, u32[]{:S(2)}, u32[]{:S(2)}) collective-permute-start(f32[1,8,128]{2,1,0:T(8,128)S(1)} %slice.884), channel_id=1, source_target_pairs={{16,0},{32,16},{48,32},{64,48},{80,64},{96,80},{112,96},{128,112},... | collective-permute-start | bytes 12296 | tf_op jit(solution)/shard_map/ppermute | solution.py:26
  24.6 92.3 %collective-permute-start.5 = (f32[1,8,128]{2,1,0:T(8,128)S(1)}, f32[1,8,128]{2,1,0:T(8,128)S(1)}, u32[]{:S(2)}, u32[]{:S(2)}) collective-permute-start(f32[1,8,128]{2,1,0:T(8,128)S(1)} %get-tuple-element.212), channel_id=1, source_target_pairs={{16,0},{32,16},{48,32},{64,48},{80,64},{96,80},{112,96},{128,112},... | collective-permute-start | bytes 12296 | tf_op jit(solution)/shard_map/ppermute | solution.py:26
  147.3 47.9 %collective-permute-start.6 = (f32[1,8,128]{2,1,0:T(8,128)S(1)}, f32[1,8,128]{2,1,0:T(8,128)S(1)}, u32[]{:S(2)}, u32[]{:S(2)}) collective-permute-start(f32[1,8,128]{2,1,0:T(8,128)S(1)} %fusion.18), channel_id=1, source_target_pairs={{0,16},{16,32},{32,48},{48,64},{64,80},{80,96},{96,112},{112,128},... | collective-permute-start | bytes 12296 | tf_op jit(solution)/shard_map/ppermute | solution.py:26
  149.0 55.4 %all-to-all-start.1 = ((f32[32,8,128]{2,1,0:T(8,128)}), f32[32,8,128]{2,1,0:T(8,128)S(1)}, u32[]{:S(2)}, u32[]{:S(2)}) async-start(f32[32,8,128]{2,1,0:T(8,128)} %param.4), calls=%async_computation.1 | async-start | bytes 262144 | tf_op jit(solution)/shard_map/all_to_all | solution.py:163
  204.4 11.9 %all-to-all-start = ((f32[32,8,128]{2,1,0:T(8,128)}), f32[32,8,128]{2,1,0:T(8,128)S(1)}, u32[]{:S(2)}, u32[]{:S(2)}) async-start(f32[32,8,128]{2,1,0:T(8,128)} %fusion.9), calls=%async_computation | async-start | bytes 262144 | tf_op jit(solution)/shard_map/all_to_all | solution.py:162
